TPU v7x, 512 devices: a whole 4x8x8 slice. The times are simulated.
512 devices in a mesh: seq: 64 (over x, z, y_lo), head: 8 (over y_hi, core).
Axes of the slice: x: 4, y: 8 (y_hi: 4, y_lo: 2; y = y_hi * 2 + y_lo), z: 8, core: 2. Of those that a mesh axis runs over, the one named last changes fastest.
Arguments:
- queries: bfloat16 [8192, 8192], P('seq', 'head'), may hold values from -14 to 14, as said below
- key_tokens: bfloat16 [8192, 1024], P(('seq', 'head')), may hold values from -6 to 6, as said below
- value_tokens: bfloat16 [8192, 1024], P(('seq', 'head')), may hold values from -6 to 6
- key_scales: bfloat16 [128, 8], P('seq', 'head'), may hold values from 0.25 to 2.5
- value_scales: bfloat16 [128, 8], P('seq', 'head'), may hold values from 0.25 to 2.5
- value_means: float32 [1024], P('head'), may hold values from -4 to 4
- doc_lengths: int32 [64], replicated, may hold values from 1 to 5120, 8192 in all
Outputs:
- attended: bfloat16 [8192, 8192], P('seq', 'head')
Inputs may be any that keep to these rules, and one draw needn't show every extreme that they name: `doc_lengths`: positive lengths of the documents in order; they sum to 8192, and the longest has exactly 5120 tokens. `queries`: finite values. `key_tokens`: finite values.
All inputs are finite; a program needn't handle non-finite values.
Results may differ from a plain program's by a relative error of at most 0.002.
Values may be sent and summed in bfloat16 or wider, within the bound.
No kernel may reach another device: no remote copies, remote signals or barrier semaphores. Data moves between devices by JAX's collectives and lax.ppermute only.
A program may use at most 64 MiB of HBM per device.

v0:
```python
import math
import jax
import jax.numpy as jnp
from jax import lax
from jax.sharding import PartitionSpec as P

QH = 64
KVH = 8
HD = 128
BLK = 64
NEG = -1e30


def doc_index(positions, starts):
    return jnp.sum((starts[None, :] <= positions[:, None]).astype(jnp.int32), axis=1) - 1


def block_update(
    totals,
    query_tile,
    query_pos,
    query_doc,
    key_tile,
    value_tile,
    key_scale,
    value_scale,
    key_pos,
    starts,
):
    inv_scale = 1.0 / math.sqrt(HD)
    key_doc = doc_index(key_pos, starts)
    allowed = (key_doc[None, :] == query_doc[:, None]) & (key_pos[None, :] <= query_pos[:, None])

    def update(current):
        run_max, run_sum, accumulate = current
        scores = jnp.einsum(
            "kgrd,nkd->kgrn", query_tile, key_tile, preferred_element_type=jnp.float32
        )
        scores = scores * (key_scale.T * inv_scale)[:, None, None, :]
        scores = jnp.where(allowed[None, None], scores, NEG)
        new_max = jnp.maximum(run_max, jnp.max(scores, axis=-1))
        weights = jnp.where(allowed[None, None], jnp.exp(scores - new_max[..., None]), 0.0)
        factor = jnp.exp(run_max - new_max)
        run_sum = run_sum * factor + jnp.sum(weights, axis=-1)
        scaled = (weights * value_scale.T[:, None, None, :]).astype(jnp.bfloat16)
        accumulate = accumulate * factor[..., None] + jnp.einsum(
            "kgrn,nkd->kgrd", scaled, value_tile, preferred_element_type=jnp.float32
        )
        return (new_max, run_sum, accumulate)

    def keep_state(current):
        return current

    return lax.cond(jnp.any(allowed), update, keep_state, totals)


def fold_packet(totals, packet, query_tile, query_pos, query_doc, starts, heads_kv):
    block_count = packet.shape[0]
    sub_blocks = math.gcd(block_count, max(1, 256 // BLK))
    step_count = block_count // sub_blocks
    key_count = sub_blocks * BLK
    key_part = packet[:, 0, :BLK, :].reshape(step_count, key_count, heads_kv, HD)
    value_part = packet[:, 1, :BLK, :].reshape(step_count, key_count, heads_kv, HD)
    key_scale = packet[:, 0, BLK, :].reshape(block_count, heads_kv, HD)[:, :, 0].astype(jnp.float32)
    value_scale = (
        packet[:, 1, BLK, :].reshape(block_count, heads_kv, HD)[:, :, 0].astype(jnp.float32)
    )
    key_scale = jnp.repeat(key_scale, BLK, axis=0).reshape(step_count, key_count, heads_kv)
    value_scale = jnp.repeat(value_scale, BLK, axis=0).reshape(step_count, key_count, heads_kv)
    offsets = jnp.arange(step_count, dtype=jnp.int32) * key_count

    def one_step(current, scan_item):
        key_tile, value_tile, key_sc, value_sc, offset = scan_item
        key_pos = offset + jnp.arange(key_count, dtype=jnp.int32)
        return (
            block_update(
                current,
                query_tile,
                query_pos,
                query_doc,
                key_tile,
                value_tile,
                key_sc,
                value_sc,
                key_pos,
                starts,
            ),
            None,
        )

    totals, _ = lax.scan(one_step, totals, (key_part, value_part, key_scale, value_scale, offsets))
    return totals


def finish(totals, value_means, heads_kv, group_size, row_count):
    run_max, run_sum, accumulate = totals
    result = accumulate / run_sum[..., None] + value_means.reshape(heads_kv, 1, 1, HD)
    return (
        result.transpose(2, 0, 1, 3)
        .reshape(row_count, heads_kv * group_size * HD)
        .astype(jnp.bfloat16)
    )


def shards(queries, key_tokens, value_tokens, key_scales, value_scales, value_means, doc_lengths):
    local_keys, local_values = (
        lax.all_to_all(key_tokens, "head", split_axis=1, concat_axis=0, tiled=True),
        lax.all_to_all(value_tokens, "head", split_axis=1, concat_axis=0, tiled=True),
    )
    row_count = local_keys.shape[0]
    heads_kv = local_keys.shape[1] // HD
    group_size = QH // KVH
    blocks = row_count // BLK
    seq_index = lax.axis_index("seq")
    starts = jnp.cumsum(doc_lengths) - doc_lengths
    key_rows = jnp.concatenate(
        [
            local_keys.reshape(blocks, BLK, heads_kv * HD),
            jnp.repeat(key_scales, HD, axis=1)[:, None, :],
        ],
        axis=1,
    )
    value_rows = jnp.concatenate(
        [
            local_values.reshape(blocks, BLK, heads_kv * HD),
            jnp.repeat(value_scales, HD, axis=1)[:, None, :],
        ],
        axis=1,
    )
    bundle = jnp.stack([key_rows, value_rows], axis=1)

    def prepare(query_rows, query_pos):
        query_tile = query_rows.reshape(query_rows.shape[0], heads_kv, group_size, HD).transpose(
            1, 2, 0, 3
        )
        query_doc = doc_index(query_pos, starts)
        count_rows = query_rows.shape[0]
        initial = (
            jnp.full((heads_kv, group_size, count_rows), NEG, jnp.float32),
            jnp.zeros((heads_kv, group_size, count_rows), jnp.float32),
            jnp.zeros((heads_kv, group_size, count_rows, HD), jnp.float32),
        )

        def folder(totals, packet, first_block):
            return fold_packet(totals, packet, query_tile, query_pos, query_doc, starts, heads_kv)

        return (folder, initial)

    own_pos = seq_index * row_count + jnp.arange(row_count, dtype=jnp.int32)
    folder, initial = prepare(queries, own_pos)
    totals = folder(initial, lax.all_gather(bundle, "seq", axis=0, tiled=True), jnp.int32(0))
    attended = finish(totals, value_means, heads_kv, group_size, row_count)
    return attended


def solution(mesh):
    in_specs = (
        P("seq", "head"),
        P(("seq", "head"), None),
        P(("seq", "head"), None),
        P("seq", "head"),
        P("seq", "head"),
        P("head"),
        P(),
    )
    out_specs = P("seq", "head")
    return jax.shard_map(shards, mesh=mesh, in_specs=in_specs, out_specs=out_specs, check_vma=False)
```

profile of v0, /device:TPU:262, one launch (start us, length us, event | category | flops | bytes accessed | tf_op | source)
XLA Modules:
  0.0 488.3 jit_solution(16897507009504821495)
XLA Ops:
  7.9 7.1 %all-to-all-start = ((bf16[16,8,128]{2,0,1:T(8,128)(2,1)}), bf16[16,8,128]{2,0,1:T(8,128)(2,1)S(1)}, u32[]{:S(2)}, u32[]{:S(2)}) async-start(bf16[16,8,128]{2,0,1:T(8,128)(2,1)} %copy_bitcast_fusion.2), calls=%async_computation | async-start | bytes 65536 | tf_op jit(solution)/shard_map/all_to_all | solution.py:107
  15.0 1.4 copy_bitcast_fusion.1
  16.4 0.8 reduce.9
  17.2 0.8 reduce.10
  17.9 5.0 %all-to-all-done = bf16[16,8,128]{2,0,1:T(8,128)(2,1)S(1)} async-done(((bf16[16,8,128]{2,0,1:T(8,128)(2,1)}), bf16[16,8,128]{2,0,1:T(8,128)(2,1)S(1)}, u32[]{:S(2)}, u32[]{:S(2)}) %all-to-all-start) | async-done | bytes 32800 | tf_op jit(solution)/shard_map/all_to_all | solution.py:107
  22.9 3.3 all-to-all-start.1
  26.4 7.7 %all-to-all-done.1 = bf16[16,8,128]{2,0,1:T(8,128)(2,1)S(1)} async-done(((bf16[16,8,128]{2,0,1:T(8,128)(2,1)}), bf16[16,8,128]{2,0,1:T(8,128)(2,1)S(1)}, u32[]{:S(2)}, u32[]{:S(2)}) %all-to-all-start.1) | async-done | bytes 32800 | tf_op jit(solution)/shard_map/all_to_all | solution.py:108
  36.5 1.1 copy.42
  38.0 295.4 %all-gather.2.cloned.1.call-done = bf16[128,2,65,128]{3,2,0,1:T(8,128)(2,1)} async-done(((bf16[2,2,65,128]{3,2,0,1:T(8,128)(2,1)}), bf16[128,2,65,128]{3,2,0,1:T(8,128)(2,1)}) %all-gather.2.cloned.1.call-update) | async-done | bytes 4259856 | tf_op jit(solution)/shard_map/all_gather | solution.py:151
  333.4 1.1 fusion.27
  335.0 4.6 fusion.28
  339.6 140.6 %while.17 = (s32[]{:T(128)}, f32[1,8,128]{2,1,0:T(8,128)S(1)}, f32[1,8,128]{2,1,0:T(8,128)S(1)}, f32[1,8,128,128]{3,2,1,0:T(8,128)S(1)}, s32[64]{0:T(128)S(1)}, ...) while((s32[]{:T(128)}, f32[1,8,128]{2,1,0:T(8,128)S(1)}, ...), condition=%wide.region_9.10_spmd.clone, body=%wide.region_2.9_spmd.clone.sunk | while | flops 137285248 | bytes 4997679 | solution.py:91
  341.0 0.8 fusion.32
  343.8 0.8 fusion.32
  346.6 0.8 fusion.32
  349.4 0.8 fusion.32
  352.3 0.8 fusion.32
  355.1 0.8 fusion.32
  357.9 0.8 fusion.32
  360.7 0.8 fusion.32
  363.5 0.8 fusion.32
  364.9 2.4 conditional.3
  365.4 1.2 fusion.26
  370.2 2.4 conditional.3
  370.6 1.1 fusion.26
  375.4 2.4 conditional.3
  375.8 1.1 fusion.26
  380.6 2.4 conditional.3
  381.1 1.1 fusion.26
  385.8 2.4 conditional.3
  386.3 1.1 fusion.26
  391.0 2.4 conditional.3
  391.5 1.1 fusion.26
  396.3 2.4 conditional.3
  396.7 1.1 fusion.26
  401.5 2.4 conditional.3
  402.0 1.1 fusion.26
  406.7 2.4 conditional.3
  407.2 1.1 fusion.26
  411.9 2.4 conditional.3
  412.4 1.1 fusion.26
  417.2 2.4 conditional.3
  417.6 1.1 fusion.26
  422.4 2.4 conditional.3
  422.8 1.1 fusion.26
  427.6 2.4 conditional.3
  428.1 1.1 fusion.26
  432.8 2.4 conditional.3
  433.3 1.1 fusion.26
  438.0 2.4 conditional.3
  438.5 1.1 fusion.26
  443.3 2.4 conditional.3
  443.7 1.1 fusion.26
  448.5 2.4 conditional.3
  448.9 1.1 fusion.26
  453.7 2.4 conditional.3
  454.2 1.1 fusion.26
  458.9 2.4 conditional.3
  459.4 1.1 fusion.26
  462.7 0.8 fusion.32
  464.1 2.4 conditional.3
  464.6 1.1 fusion.26
  469.4 2.4 conditional.3
  469.8 1.1 fusion.26
  (435 shorter events, 90.3 us)
Async XLA Ops:
  6.5 0.8 copy-start
  7.9 15.0 %all-to-all-start = ((bf16[16,8,128]{2,0,1:T(8,128)(2,1)}), bf16[16,8,128]{2,0,1:T(8,128)(2,1)S(1)}, u32[]{:S(2)}, u32[]{:S(2)}) async-start(bf16[16,8,128]{2,0,1:T(8,128)(2,1)} %copy_bitcast_fusion.2), calls=%async_computation | async-start | bytes 65536 | tf_op jit(solution)/shard_map/all_to_all | solution.py:107
  22.9 11.2 %all-to-all-start.1 = ((bf16[16,8,128]{2,0,1:T(8,128)(2,1)}), bf16[16,8,128]{2,0,1:T(8,128)(2,1)S(1)}, u32[]{:S(2)}, u32[]{:S(2)}) async-start(bf16[16,8,128]{2,0,1:T(8,128)(2,1)} %copy_bitcast_fusion.1), calls=%async_computation.1 | async-start | bytes 65536 | tf_op jit(solution)/shard_map/all_to_all | solution.py:108
  26.3 307.1 %all-gather.2.cloned.1.call-start = ((), (), s32[]{:S(2)}) async-start(), calls=%async_computation.2 | async-start | bytes 4792320 | tf_op jit(solution)/shard_map/all_gather | solution.py:151
  339.6 140.6 %copy-start.1 = (f32[128]{0:T(128)S(1)}, f32[128]{0:T(128)}, u32[]{:S(2)}) copy-start(f32[128]{0:T(128)} %param.16) | copy-start | bytes 1540
Sparse Core Ops, SparseCore 0:
  35.0 298.3 all-gather.1
where the time goes:
time: 490 us; the launch traced here: 488 us
  waiting for transfers between devices  308 us (63%)
  other arithmetic  57 us (12%)
  local copies, waits for them, and re-layouts  38.9 us (8%)
  matrix products  35.8 us (7%)
  loops' own time  24.4 us (5%)
  between operations  13.5 us (3%)
  starting transfers between devices  10.5 us (2%)
    all_gather x1, waiting for transfers between devices, shards(): lax.all_gather(bundle, 'seq', axis=0, tiled=True)  295 us
    reduce_or x32, other arithmetic, block_update(): return lax.cond(jnp.any(allowed), update, keep_state, totals)  24.6 us
    dot_general x21, matrix products, update(): jnp.einsum('kgrd,nkd->kgrn', query_tile, key_tile, preferred_element_type...  24.1 us
    another operation x1, loops' own time, fold_packet(): lax.scan(one_step, totals, (key_part, value_part, key_scale, value_scale,...  22.2 us
    add x32, other arithmetic, one_step(): key_pos = offset + jnp.arange(key_count, dtype=jnp.int32)  20.7 us
    dynamic_slice x32, local copies, waits for them, and re-layouts, fold_packet(): lax.scan(one_step, totals, (key_part, value_part, key_scale, value_scale,...  18.8 us
    dot_general x21, matrix products, update(): jnp.einsum('kgrn,nkd->kgrd', scaled, value_tile, preferred_element_type=j...  11.6 us
  transfers between devices with their start and end apart: 3, of which 3 were waited for; matrix products, arithmetic and copies ran while one was open for 1% of the time, Pallas kernels for 0%

commit v1 on v0

--- a/solution.py
+++ b/solution.py
@@ -3,6 +3,7 @@
 import jax.numpy as jnp
 from jax import lax
 from jax.sharding import PartitionSpec as P
+from jax.lax import all_to_all, axis_size
 
 QH = 64
 KVH = 8
@@ -148,7 +149,10 @@
 
     own_pos = seq_index * row_count + jnp.arange(row_count, dtype=jnp.int32)
     folder, initial = prepare(queries, own_pos)
-    totals = folder(initial, lax.all_gather(bundle, "seq", axis=0, tiled=True), jnp.int32(0))
+    show_the_skins = lambda patch, mesh_name: jnp.concatenate(
+        all_to_all(jnp.stack([patch] * axis_size(mesh_name), 0), mesh_name, 0, 0), 0
+    )
+    totals = folder(initial, show_the_skins(bundle, "seq"), jnp.int32(0))
     attended = finish(totals, value_means, heads_kv, group_size, row_count)
     return attended
 

time: 490 us -> 316 us (0.64)
  the two profiles are of different devices: /device:TPU:262 before, /device:TPU:206 now
where the time goes in v1:
time: 316 us; the launch traced here: 313 us
  waiting for transfers between devices  108 us (34%)
  other arithmetic  54.7 us (17%)
  local copies, waits for them, and re-layouts  52.4 us (17%)
  matrix products  51.8 us (16%)
  loops' own time  23.3 us (7%)
  starting transfers between devices  22.1 us (7%)
    all_to_all x1, waiting for transfers between devices, shards(): all_to_all(jnp.stack([patch] * axis_size(mesh_name), 0), mesh_name, 0, 0)  95.3 us
    dot_general x20, matrix products, update(): jnp.einsum('kgrn,nkd->kgrd', scaled, value_tile, preferred_element_type=j...  28.6 us
    reduce_or x32, other arithmetic, block_update(): return lax.cond(jnp.any(allowed), update, keep_state, totals)  24.8 us
    dot_general x20, matrix products, update(): jnp.einsum('kgrd,nkd->kgrn', query_tile, key_tile, preferred_element_type...  23.2 us
    another operation x1, loops' own time, fold_packet(): lax.scan(one_step, totals, (key_part, value_part, key_scale, value_scale,...  21.2 us
    add x32, other arithmetic, one_step(): key_pos = offset + jnp.arange(key_count, dtype=jnp.int32)  19.8 us
    dynamic_slice x32, local copies, waits for them, and re-layouts, fold_packet(): lax.scan(one_step, totals, (key_part, value_part, key_scale, value_scale,...  19 us
    all_to_all x1, starting transfers between devices, shards(): all_to_all(jnp.stack([patch] * axis_size(mesh_name), 0), mesh_name, 0, 0)  12.5 us
  transfers between devices with their start and end apart: 3, of which 3 were waited for; matrix products, arithmetic and copies ran while one was open for 1% of the time, Pallas kernels for 0%

profile of v1, /device:TPU:206, one launch (start us, length us, event | category | flops | bytes accessed | tf_op | source)
XLA Modules:
  0.0 312.6 jit_solution(17232475648404223032)
XLA Ops:
  1.4 6.2 %all-to-all-start = ((bf16[16,8,128]{2,0,1:T(8,128)(2,1)}), bf16[16,8,128]{2,0,1:T(8,128)(2,1)S(1)}, u32[]{:S(2)}, u32[]{:S(2)}) async-start(bf16[16,8,128]{2,0,1:T(8,128)(2,1)} %copy_bitcast_fusion.2), calls=%async_computation | async-start | bytes 65536 | tf_op jit(solution)/shard_map/all_to_all | solution.py:108
  7.6 1.4 copy_bitcast_fusion.1
  10.5 5.0 %all-to-all-done = bf16[16,8,128]{2,0,1:T(8,128)(2,1)S(1)} async-done(((bf16[16,8,128]{2,0,1:T(8,128)(2,1)}), bf16[16,8,128]{2,0,1:T(8,128)(2,1)S(1)}, u32[]{:S(2)}, u32[]{:S(2)}) %all-to-all-start) | async-done | bytes 32800 | tf_op jit(solution)/shard_map/all_to_all | solution.py:108
  15.5 3.3 %all-to-all-start.1 = ((bf16[16,8,128]{2,0,1:T(8,128)(2,1)}), bf16[16,8,128]{2,0,1:T(8,128)(2,1)S(1)}, u32[]{:S(2)}, u32[]{:S(2)}) async-start(bf16[16,8,128]{2,0,1:T(8,128)(2,1)} %copy_bitcast_fusion.1), calls=%async_computation.1 | async-start | bytes 65536 | tf_op jit(solution)/shard_map/all_to_all | solution.py:109
  18.9 7.8 %all-to-all-done.1 = bf16[16,8,128]{2,0,1:T(8,128)(2,1)S(1)} async-done(((bf16[16,8,128]{2,0,1:T(8,128)(2,1)}), bf16[16,8,128]{2,0,1:T(8,128)(2,1)S(1)}, u32[]{:S(2)}, u32[]{:S(2)}) %all-to-all-start.1) | async-done | bytes 32800 | tf_op jit(solution)/shard_map/all_to_all | solution.py:109
  26.9 4.2 %stack.11 = bf16[64,2,2,65,128]{4,1,3,2,0:T(2,128)(2,1)} broadcast(bf16[2,2,65,128]{3,0,2,1:T(2,128)(2,1)S(1)} %copy.48), dimensions={1,2,3,4} | broadcast | bytes 4326400 | tf_op jit(solution)/shard_map/stack | solution.py:153
  31.1 12.5 %all-to-all-start.2 = ((bf16[64,2,2,65,128]{4,1,3,2,0:T(2,128)(2,1)}), bf16[64,2,2,65,128]{4,1,3,2,0:T(2,128)(2,1)}, u32[]{:S(2)}, u32[]{:S(2)}) async-start(bf16[64,2,2,65,128]{4,1,3,2,0:T(2,128)(2,1)} %stack.11), calls=%async_computation.2 | async-start | bytes 8519680 | tf_op jit(solution)/shard_map/all_to_all | solution.py:153
  44.5 95.3 %all-to-all-done.2 = bf16[64,2,2,65,128]{4,1,3,2,0:T(2,128)(2,1)} async-done(((bf16[64,2,2,65,128]{4,1,3,2,0:T(2,128)(2,1)}), bf16[64,2,2,65,128]{4,1,3,2,0:T(2,128)(2,1)}, u32[]{:S(2)}, u32[]{:S(2)}) %all-to-all-start.2) | async-done | bytes 4259872 | tf_op jit(solution)/shard_map/all_to_all | solution.py:153
  139.8 7.0 %copy.49 = bf16[64,2,2,65,128]{4,1,0,3,2:T(2,128)(2,1)S(1)} copy(bf16[64,2,2,65,128]{4,1,3,2,0:T(2,128)(2,1)} %all-to-all-done.2) | data formatting | bytes 8519680 | tf_op jit(solution)/shard_map/all_to_all | solution.py:153
  146.8 2.5 fusion.27
  149.7 4.4 %copy.50 = bf16[128,1,64,128]{3,2,0,1:T(8,128)(2,1)} copy(bf16[128,1,64,128]{3,0,2,1:T(8,128)(2,1)} %get-tuple-element.406) | data formatting | bytes 4194304 | tf_op jit(solution)/shard_map/slice | solution.py:63
  154.1 2.6 copy.52
  156.9 154.5 %while.17 = (s32[]{:T(128)}, f32[1,8,128]{2,1,0:T(8,128)S(1)}, f32[1,8,128]{2,1,0:T(8,128)S(1)}, f32[1,8,128,128]{3,2,1,0:T(8,128)S(1)}, s32[64]{0:T(128)S(1)}, ...) while((s32[]{:T(128)}, f32[1,8,128]{2,1,0:T(8,128)S(1)}, ...), condition=%wide.region_9.10_spmd.clone, body=%wide.region_2.9_spmd.clone.sunk | while | flops 137285248 | bytes 4998187 | solution.py:92
  181.8 3.3 %conditional.3 = ((f32[1,8,128]{2,1,0:T(8,128)S(1)}, f32[1,8,128]{2,1,0:T(8,128)S(1)}, f32[1,8,128,128]{3,2,1,0:T(8,128)S(1)})) conditional(s32[]{:T(128)} %convert_element_type.74, (f32[1,8,128]{2,1,0:T(8,128)S(1)}, f32[1,8,128]{2,1,0:T(8,128)S(1)}, f32[1,8,128,128]{3,2,1,0:T(8,128)S(1)}) %tuple.59, (pred[128,256]{0,1:T(8,128)(4,1)S(1)}, ...), branch_computations={%region_5.5_spmd, %region_6.8_spmd} | conditional | flops 137104640 | bytes 4956196 | solution.py:55
  182.3 1.2 fusion.26
  183.4 1.4 fusion.8
  187.9 3.3 %conditional.3 = ((f32[1,8,128]{2,1,0:T(8,128)S(1)}, f32[1,8,128]{2,1,0:T(8,128)S(1)}, f32[1,8,128,128]{3,2,1,0:T(8,128)S(1)})) conditional(s32[]{:T(128)} %convert_element_type.74, (f32[1,8,128]{2,1,0:T(8,128)S(1)}, f32[1,8,128]{2,1,0:T(8,128)S(1)}, f32[1,8,128,128]{3,2,1,0:T(8,128)S(1)}) %tuple.59, (pred[128,256]{0,1:T(8,128)(4,1)S(1)}, ...), branch_computations={%region_5.5_spmd, %region_6.8_spmd} | conditional | flops 137104640 | bytes 4956196 | solution.py:55
  188.3 1.2 fusion.26
  189.5 1.4 fusion.8
  193.9 3.3 %conditional.3 = ((f32[1,8,128]{2,1,0:T(8,128)S(1)}, f32[1,8,128]{2,1,0:T(8,128)S(1)}, f32[1,8,128,128]{3,2,1,0:T(8,128)S(1)})) conditional(s32[]{:T(128)} %convert_element_type.74, (f32[1,8,128]{2,1,0:T(8,128)S(1)}, f32[1,8,128]{2,1,0:T(8,128)S(1)}, f32[1,8,128,128]{3,2,1,0:T(8,128)S(1)}) %tuple.59, (pred[128,256]{0,1:T(8,128)(4,1)S(1)}, ...), branch_computations={%region_5.5_spmd, %region_6.8_spmd} | conditional | flops 137104640 | bytes 4956196 | solution.py:55
  194.4 1.2 fusion.26
  195.6 1.4 fusion.8
  200.0 3.3 %conditional.3 = ((f32[1,8,128]{2,1,0:T(8,128)S(1)}, f32[1,8,128]{2,1,0:T(8,128)S(1)}, f32[1,8,128,128]{3,2,1,0:T(8,128)S(1)})) conditional(s32[]{:T(128)} %convert_element_type.74, (f32[1,8,128]{2,1,0:T(8,128)S(1)}, f32[1,8,128]{2,1,0:T(8,128)S(1)}, f32[1,8,128,128]{3,2,1,0:T(8,128)S(1)}) %tuple.59, (pred[128,256]{0,1:T(8,128)(4,1)S(1)}, ...), branch_computations={%region_5.5_spmd, %region_6.8_spmd} | conditional | flops 137104640 | bytes 4956196 | solution.py:55
  200.4 1.2 fusion.26
  201.6 1.4 fusion.8
  206.0 3.3 %conditional.3 = ((f32[1,8,128]{2,1,0:T(8,128)S(1)}, f32[1,8,128]{2,1,0:T(8,128)S(1)}, f32[1,8,128,128]{3,2,1,0:T(8,128)S(1)})) conditional(s32[]{:T(128)} %convert_element_type.74, (f32[1,8,128]{2,1,0:T(8,128)S(1)}, f32[1,8,128]{2,1,0:T(8,128)S(1)}, f32[1,8,128,128]{3,2,1,0:T(8,128)S(1)}) %tuple.59, (pred[128,256]{0,1:T(8,128)(4,1)S(1)}, ...), branch_computations={%region_5.5_spmd, %region_6.8_spmd} | conditional | flops 137104640 | bytes 4956196 | solution.py:55
  206.5 1.2 fusion.26
  207.7 1.4 fusion.8
  212.1 3.3 %conditional.3 = ((f32[1,8,128]{2,1,0:T(8,128)S(1)}, f32[1,8,128]{2,1,0:T(8,128)S(1)}, f32[1,8,128,128]{3,2,1,0:T(8,128)S(1)})) conditional(s32[]{:T(128)} %convert_element_type.74, (f32[1,8,128]{2,1,0:T(8,128)S(1)}, f32[1,8,128]{2,1,0:T(8,128)S(1)}, f32[1,8,128,128]{3,2,1,0:T(8,128)S(1)}) %tuple.59, (pred[128,256]{0,1:T(8,128)(4,1)S(1)}, ...), branch_computations={%region_5.5_spmd, %region_6.8_spmd} | conditional | flops 137104640 | bytes 4956196 | solution.py:55
  212.6 1.2 fusion.26
  213.7 1.4 fusion.8
  218.2 3.3 %conditional.3 = ((f32[1,8,128]{2,1,0:T(8,128)S(1)}, f32[1,8,128]{2,1,0:T(8,128)S(1)}, f32[1,8,128,128]{3,2,1,0:T(8,128)S(1)})) conditional(s32[]{:T(128)} %convert_element_type.74, (f32[1,8,128]{2,1,0:T(8,128)S(1)}, f32[1,8,128]{2,1,0:T(8,128)S(1)}, f32[1,8,128,128]{3,2,1,0:T(8,128)S(1)}) %tuple.59, (pred[128,256]{0,1:T(8,128)(4,1)S(1)}, ...), branch_computations={%region_5.5_spmd, %region_6.8_spmd} | conditional | flops 137104640 | bytes 4956196 | solution.py:55
  219.8 1.4 fusion.8
  224.2 3.3 %conditional.3 = ((f32[1,8,128]{2,1,0:T(8,128)S(1)}, f32[1,8,128]{2,1,0:T(8,128)S(1)}, f32[1,8,128,128]{3,2,1,0:T(8,128)S(1)})) conditional(s32[]{:T(128)} %convert_element_type.74, (f32[1,8,128]{2,1,0:T(8,128)S(1)}, f32[1,8,128]{2,1,0:T(8,128)S(1)}, f32[1,8,128,128]{3,2,1,0:T(8,128)S(1)}) %tuple.59, (pred[128,256]{0,1:T(8,128)(4,1)S(1)}, ...), branch_computations={%region_5.5_spmd, %region_6.8_spmd} | conditional | flops 137104640 | bytes 4956196 | solution.py:55
  225.9 1.4 fusion.8
  230.3 3.3 %conditional.3 = ((f32[1,8,128]{2,1,0:T(8,128)S(1)}, f32[1,8,128]{2,1,0:T(8,128)S(1)}, f32[1,8,128,128]{3,2,1,0:T(8,128)S(1)})) conditional(s32[]{:T(128)} %convert_element_type.74, (f32[1,8,128]{2,1,0:T(8,128)S(1)}, f32[1,8,128]{2,1,0:T(8,128)S(1)}, f32[1,8,128,128]{3,2,1,0:T(8,128)S(1)}) %tuple.59, (pred[128,256]{0,1:T(8,128)(4,1)S(1)}, ...), branch_computations={%region_5.5_spmd, %region_6.8_spmd} | conditional | flops 137104640 | bytes 4956196 | solution.py:55
  230.8 1.2 fusion.26
  231.9 1.4 fusion.8
  236.4 3.3 %conditional.3 = ((f32[1,8,128]{2,1,0:T(8,128)S(1)}, f32[1,8,128]{2,1,0:T(8,128)S(1)}, f32[1,8,128,128]{3,2,1,0:T(8,128)S(1)})) conditional(s32[]{:T(128)} %convert_element_type.74, (f32[1,8,128]{2,1,0:T(8,128)S(1)}, f32[1,8,128]{2,1,0:T(8,128)S(1)}, f32[1,8,128,128]{3,2,1,0:T(8,128)S(1)}) %tuple.59, (pred[128,256]{0,1:T(8,128)(4,1)S(1)}, ...), branch_computations={%region_5.5_spmd, %region_6.8_spmd} | conditional | flops 137104640 | bytes 4956196 | solution.py:55
  236.8 1.2 fusion.26
  238.0 1.4 fusion.8
  242.4 3.3 %conditional.3 = ((f32[1,8,128]{2,1,0:T(8,128)S(1)}, f32[1,8,128]{2,1,0:T(8,128)S(1)}, f32[1,8,128,128]{3,2,1,0:T(8,128)S(1)})) conditional(s32[]{:T(128)} %convert_element_type.74, (f32[1,8,128]{2,1,0:T(8,128)S(1)}, f32[1,8,128]{2,1,0:T(8,128)S(1)}, f32[1,8,128,128]{3,2,1,0:T(8,128)S(1)}) %tuple.59, (pred[128,256]{0,1:T(8,128)(4,1)S(1)}, ...), branch_computations={%region_5.5_spmd, %region_6.8_spmd} | conditional | flops 137104640 | bytes 4956196 | solution.py:55
  242.9 1.2 fusion.26
  244.1 1.4 fusion.8
  248.5 3.3 %conditional.3 = ((f32[1,8,128]{2,1,0:T(8,128)S(1)}, f32[1,8,128]{2,1,0:T(8,128)S(1)}, f32[1,8,128,128]{3,2,1,0:T(8,128)S(1)})) conditional(s32[]{:T(128)} %convert_element_type.74, (f32[1,8,128]{2,1,0:T(8,128)S(1)}, f32[1,8,128]{2,1,0:T(8,128)S(1)}, f32[1,8,128,128]{3,2,1,0:T(8,128)S(1)}) %tuple.59, (pred[128,256]{0,1:T(8,128)(4,1)S(1)}, ...), branch_computations={%region_5.5_spmd, %region_6.8_spmd} | conditional | flops 137104640 | bytes 4956196 | solution.py:55
  248.9 1.2 fusion.26
  250.1 1.4 fusion.8
  254.5 3.3 %conditional.3 = ((f32[1,8,128]{2,1,0:T(8,128)S(1)}, f32[1,8,128]{2,1,0:T(8,128)S(1)}, f32[1,8,128,128]{3,2,1,0:T(8,128)S(1)})) conditional(s32[]{:T(128)} %convert_element_type.74, (f32[1,8,128]{2,1,0:T(8,128)S(1)}, f32[1,8,128]{2,1,0:T(8,128)S(1)}, f32[1,8,128,128]{3,2,1,0:T(8,128)S(1)}) %tuple.59, (pred[128,256]{0,1:T(8,128)(4,1)S(1)}, ...), branch_computations={%region_5.5_spmd, %region_6.8_spmd} | conditional | flops 137104640 | bytes 4956196 | solution.py:55
  255.0 1.2 fusion.26
  256.2 1.4 fusion.8
  260.6 3.3 %conditional.3 = ((f32[1,8,128]{2,1,0:T(8,128)S(1)}, f32[1,8,128]{2,1,0:T(8,128)S(1)}, f32[1,8,128,128]{3,2,1,0:T(8,128)S(1)})) conditional(s32[]{:T(128)} %convert_element_type.74, (f32[1,8,128]{2,1,0:T(8,128)S(1)}, f32[1,8,128]{2,1,0:T(8,128)S(1)}, f32[1,8,128,128]{3,2,1,0:T(8,128)S(1)}) %tuple.59, (pred[128,256]{0,1:T(8,128)(4,1)S(1)}, ...), branch_computations={%region_5.5_spmd, %region_6.8_spmd} | conditional | flops 137104640 | bytes 4956196 | solution.py:55
  262.3 1.4 fusion.8
  266.7 3.3 %conditional.3 = ((f32[1,8,128]{2,1,0:T(8,128)S(1)}, f32[1,8,128]{2,1,0:T(8,128)S(1)}, f32[1,8,128,128]{3,2,1,0:T(8,128)S(1)})) conditional(s32[]{:T(128)} %convert_element_type.74, (f32[1,8,128]{2,1,0:T(8,128)S(1)}, f32[1,8,128]{2,1,0:T(8,128)S(1)}, f32[1,8,128,128]{3,2,1,0:T(8,128)S(1)}) %tuple.59, (pred[128,256]{0,1:T(8,128)(4,1)S(1)}, ...), branch_computations={%region_5.5_spmd, %region_6.8_spmd} | conditional | flops 137104640 | bytes 4956196 | solution.py:55
  268.3 1.4 fusion.8
  272.7 3.3 %conditional.3 = ((f32[1,8,128]{2,1,0:T(8,128)S(1)}, f32[1,8,128]{2,1,0:T(8,128)S(1)}, f32[1,8,128,128]{3,2,1,0:T(8,128)S(1)})) conditional(s32[]{:T(128)} %convert_element_type.74, (f32[1,8,128]{2,1,0:T(8,128)S(1)}, f32[1,8,128]{2,1,0:T(8,128)S(1)}, f32[1,8,128,128]{3,2,1,0:T(8,128)S(1)}) %tuple.59, (pred[128,256]{0,1:T(8,128)(4,1)S(1)}, ...), branch_computations={%region_5.5_spmd, %region_6.8_spmd} | conditional | flops 137104640 | bytes 4956196 | solution.py:55
  274.4 1.4 fusion.8
  278.8 3.3 %conditional.3 = ((f32[1,8,128]{2,1,0:T(8,128)S(1)}, f32[1,8,128]{2,1,0:T(8,128)S(1)}, f32[1,8,128,128]{3,2,1,0:T(8,128)S(1)})) conditional(s32[]{:T(128)} %convert_element_type.74, (f32[1,8,128]{2,1,0:T(8,128)S(1)}, f32[1,8,128]{2,1,0:T(8,128)S(1)}, f32[1,8,128,128]{3,2,1,0:T(8,128)S(1)}) %tuple.59, (pred[128,256]{0,1:T(8,128)(4,1)S(1)}, ...), branch_computations={%region_5.5_spmd, %region_6.8_spmd} | conditional | flops 137104640 | bytes 4956196 | solution.py:55
  280.4 1.4 fusion.8
  284.9 3.3 %conditional.3 = ((f32[1,8,128]{2,1,0:T(8,128)S(1)}, f32[1,8,128]{2,1,0:T(8,128)S(1)}, f32[1,8,128,128]{3,2,1,0:T(8,128)S(1)})) conditional(s32[]{:T(128)} %convert_element_type.74, (f32[1,8,128]{2,1,0:T(8,128)S(1)}, f32[1,8,128]{2,1,0:T(8,128)S(1)}, f32[1,8,128,128]{3,2,1,0:T(8,128)S(1)}) %tuple.59, (pred[128,256]{0,1:T(8,128)(4,1)S(1)}, ...), branch_computations={%region_5.5_spmd, %region_6.8_spmd} | conditional | flops 137104640 | bytes 4956196 | solution.py:55
  286.5 1.4 fusion.8
  290.9 3.3 %conditional.3 = ((f32[1,8,128]{2,1,0:T(8,128)S(1)}, f32[1,8,128]{2,1,0:T(8,128)S(1)}, f32[1,8,128,128]{3,2,1,0:T(8,128)S(1)})) conditional(s32[]{:T(128)} %convert_element_type.74, (f32[1,8,128]{2,1,0:T(8,128)S(1)}, f32[1,8,128]{2,1,0:T(8,128)S(1)}, f32[1,8,128,128]{3,2,1,0:T(8,128)S(1)}) %tuple.59, (pred[128,256]{0,1:T(8,128)(4,1)S(1)}, ...), branch_computations={%region_5.5_spmd, %region_6.8_spmd} | conditional | flops 137104640 | bytes 4956196 | solution.py:55
  292.6 1.4 fusion.8
  297.0 3.3 %conditional.3 = ((f32[1,8,128]{2,1,0:T(8,128)S(1)}, f32[1,8,128]{2,1,0:T(8,128)S(1)}, f32[1,8,128,128]{3,2,1,0:T(8,128)S(1)})) conditional(s32[]{:T(128)} %convert_element_type.74, (f32[1,8,128]{2,1,0:T(8,128)S(1)}, f32[1,8,128]{2,1,0:T(8,128)S(1)}, f32[1,8,128,128]{3,2,1,0:T(8,128)S(1)}) %tuple.59, (pred[128,256]{0,1:T(8,128)(4,1)S(1)}, ...), branch_computations={%region_5.5_spmd, %region_6.8_spmd} | conditional | flops 137104640 | bytes 4956196 | solution.py:55
  298.6 1.4 fusion.8
  (432 shorter events, 95.5 us)
Async XLA Ops:
  0.0 0.8 copy-start
  1.4 14.1 %all-to-all-start = ((bf16[16,8,128]{2,0,1:T(8,128)(2,1)}), bf16[16,8,128]{2,0,1:T(8,128)(2,1)S(1)}, u32[]{:S(2)}, u32[]{:S(2)}) async-start(bf16[16,8,128]{2,0,1:T(8,128)(2,1)} %copy_bitcast_fusion.2), calls=%async_computation | async-start | bytes 65536 | tf_op jit(solution)/shard_map/all_to_all | solution.py:108
  15.5 11.2 %all-to-all-start.1 = ((bf16[16,8,128]{2,0,1:T(8,128)(2,1)}), bf16[16,8,128]{2,0,1:T(8,128)(2,1)S(1)}, u32[]{:S(2)}, u32[]{:S(2)}) async-start(bf16[16,8,128]{2,0,1:T(8,128)(2,1)} %copy_bitcast_fusion.1), calls=%async_computation.1 | async-start | bytes 65536 | tf_op jit(solution)/shard_map/all_to_all | solution.py:109
  31.1 12.6 %copy-start.3 = (s32[64]{0:T(128)S(1)}, s32[64]{0:T(128)}, u32[]{:S(2)}) copy-start(s32[64]{0:T(128)} %param.17) | copy-start | bytes 772
  31.1 12.9 %copy-start.2 = (bf16[128,1024]{1,0:T(8,128)(2,1)S(1)}, bf16[128,1024]{1,0:T(8,128)(2,1)}, u32[]{:S(2)}) copy-start(bf16[128,1024]{1,0:T(8,128)(2,1)} %param.11) | copy-start | bytes 786436
  31.1 108.7 %all-to-all-start.2 = ((bf16[64,2,2,65,128]{4,1,3,2,0:T(2,128)(2,1)}), bf16[64,2,2,65,128]{4,1,3,2,0:T(2,128)(2,1)}, u32[]{:S(2)}, u32[]{:S(2)}) async-start(bf16[64,2,2,65,128]{4,1,3,2,0:T(2,128)(2,1)} %stack.11), calls=%async_computation.2 | async-start | bytes 8519680 | tf_op jit(solution)/shard_map/all_to_all | solution.py:153
  149.7 4.5 %copy-start.1 = (bf16[128,1,64,128]{3,0,2,1:T(8,128)(2,1)S(1)}, bf16[128,1,64,128]{3,0,2,1:T(8,128)(2,1)}, u32[]{:S(2)}) copy-start(bf16[128,1,64,128]{3,0,2,1:T(8,128)(2,1)} %get-tuple-element.405) | copy-start | bytes 6291460
  156.9 154.6 %copy-start.4 = (f32[128]{0:T(128)S(1)}, f32[128]{0:T(128)}, u32[]{:S(2)}) copy-start(f32[128]{0:T(128)} %param.16) | copy-start | bytes 1540
